TPU v7x, 256 devices: a whole 4x4x8 slice. The times are simulated.
256 devices in a mesh: grp: 32 (over z, y_hi, core), tp: 8 (over y_lo, x).
Axes of the slice: x: 4, y: 4 (y_hi: 2, y_lo: 2; y = y_hi * 2 + y_lo), z: 8, core: 2. Of those that a mesh axis runs over, the one named last changes fastest.
Arguments:
- states_in: bfloat16 [16384, 1536], P('grp', 'tp'), may hold values from -6 to 6
- segment_ids: int32 [16384], P('grp'), may hold values from 0 to 223, as said below
- positions: int32 [16384], P('grp'), may hold values from 0 to 1009, as said below
- attention_gain: bfloat16 [1536], P('tp'), may hold values from 0.5 to 1.5
- feedforward_gain: bfloat16 [1536], P('tp'), may hold values from 0.5 to 1.5
- query_weight: bfloat16 [1536, 1536], P('grp', 'tp'), may hold values from -1 to 1
- keyvalue_weight: bfloat16 [1536, 8, 128], P('grp', 'tp'), may hold values from -128 to 128
- output_weight: bfloat16 [1536, 1536], P('tp'), may hold values from -0.15625 to 0.15625
- route_experts: int32 [16384, 8], P('grp'), may hold values from 0 to 19, all different within a row; in each aligned block of 512 rows (0 to 511, 512 to 1023, ...) at most 256 rows name the same one
- route_weights: float32 [16384, 8], P('grp'), may hold values from 0.05 to 0.3
- expert_gateup: bfloat16 [40, 1536, 512], P('tp'), may hold values from -0.15625 to 0.15625
- expert_down: bfloat16 [40, 256, 1536], P('tp'), may hold values from -0.25 to 0.25
- cache_slots: int32 [16384], P('grp'), may hold values from 0 to 16383, as said below
Outputs:
- layer_output: bfloat16 [16384, 1536], P('grp', 'tp')
- paged_cache: bfloat16 [16384, 8, 128], P('grp', 'tp')
- log_sums: float32 [24, 16384], P('tp', 'grp')
Inputs may be any that keep to these rules, and one draw needn't show every extreme that they name: `segment_ids`: equal ids mark the tokens of one prompt; the tokens of a prompt lie within one pair of groups 2p and 2p+1. `positions`: positions count from 0 within each prompt; one prompt of groups 0 and 1 has 2 * (505) tokens. `route_experts`: each row names 8 different experts; at most 256 rows of one group name the same expert, and that number is reached. `cache_slots`: every cache row is named once; the tokens of each group fill exactly 16 rows of every group's block of 512 rows.
All inputs are finite; a program needn't handle non-finite values.
Results may differ from a plain program's by a relative error of at most 0.01.
The roundings to bfloat16 on the way count: a program that leaves them out, or rounds other values in their place, can miss the bound.
Values may be sent and summed in bfloat16 or wider, within the bound.
No kernel may reach another device: no remote copies, remote signals or barrier semaphores. Data moves between devices by JAX's collectives and lax.ppermute only.
A program may use at most 128 MiB of HBM per device.

v0:
```python
import jax
import jax.numpy as jnp
from jax import lax
from jax.sharding import Mesh
from jax.sharding import PartitionSpec as P

HD = 64
attn_scale = 0.015625
norm_eps = 1e-06
rope_base = 10000.0
G = ("z", "yh", "c")
T = ("yl", "x")


def rms_scale(values, gain_row):
    floats = values.astype(jnp.float32)
    mean_square = jnp.mean(floats * floats, axis=-1, keepdims=True)
    return (floats * lax.rsqrt(mean_square + norm_eps) * gain_row.astype(jnp.float32)).astype(
        jnp.bfloat16
    )


def rotate(values, places):
    half_width = values.shape[-1] // 2
    frequency = rope_base ** (-jnp.arange(half_width, dtype=jnp.float32) * 2.0 / values.shape[-1])
    angles = places.astype(jnp.float32)[:, None] * frequency[None, :]
    cosine = jnp.cos(angles)[:, None, :]
    sine_part = jnp.sin(angles)[:, None, :]
    leading = values[..., :half_width]
    trailing = values[..., half_width:]
    return jnp.concatenate(
        [leading * cosine - trailing * sine_part, trailing * cosine + leading * sine_part], axis=-1
    )


def attend_block(query_block, seg_block, pos_block, all_rows, all_seg, all_pos):
    key_part = all_rows[..., :HD]
    value_part = all_rows[..., HD:]
    scores = (
        jnp.einsum("qgrd,kgd->grqk", query_block, key_part, preferred_element_type=jnp.float32)
        * attn_scale
    )
    allowed = (seg_block[:, None] == all_seg[None, :]) & (all_pos[None, :] <= pos_block[:, None])
    masked = jnp.where(allowed, scores, -jnp.inf)
    row_peak = jnp.max(masked, axis=-1, keepdims=True)
    exponent = jnp.exp(masked - row_peak)
    row_total = jnp.sum(exponent, axis=-1, keepdims=True)
    log_total = (row_peak + jnp.log(row_total))[..., 0]
    weights_low = (exponent / row_total).astype(jnp.bfloat16)
    mixed_rows = jnp.einsum(
        "grqk,kgd->qgrd", weights_low, value_part, preferred_element_type=jnp.float32
    )
    return (mixed_rows.astype(jnp.bfloat16), log_total)


def expert_terms(normed, route_experts, route_weights, gateup, down, slot_first):
    local_experts = gateup.shape[0]
    half_units = down.shape[1]
    owned_experts = slot_first + jnp.arange(local_experts, dtype=jnp.int32)
    matches = route_experts[:, :, None] == owned_experts[None, None, :]
    route_scale = jnp.sum(jnp.where(matches, route_weights[:, :, None], 0.0), axis=1)
    gate_up = jnp.einsum("td,edf->etf", normed, gateup, preferred_element_type=jnp.float32)
    activated = (jax.nn.silu(gate_up[..., :half_units]) * gate_up[..., half_units:]).astype(
        jnp.bfloat16
    )
    produced = jnp.einsum("etf,efd->etd", activated, down, preferred_element_type=jnp.float32)
    return jnp.sum(route_scale.T[:, :, None] * produced, axis=0)


def gather_rows_over_groups(block):
    width = block.shape[1]
    nz = lax.axis_size("z")
    zi = lax.axis_index("z")
    got = [block]
    for k in range(1, nz):
        got.append(lax.ppermute(block, "z", [(i, (i + k) % nz) for i in range(nz)]))
    stacked = jnp.stack(got)
    zfull = jnp.take(stacked, (zi - jnp.arange(nz)) % nz, axis=0)
    yi = lax.axis_index("yh")
    other_y = lax.ppermute(zfull, "yh", [(0, 1), (1, 0)])
    yfull = jnp.where(yi == 0, jnp.stack([zfull, other_y]), jnp.stack([other_y, zfull]))
    ci = lax.axis_index("c")
    other_c = lax.ppermute(yfull, "c", [(0, 1), (1, 0)])
    cfull = jnp.where(ci == 0, jnp.stack([yfull, other_c]), jnp.stack([other_c, yfull]))
    return cfull.transpose(2, 1, 0, 3, 4).reshape(-1, width)


def shards(
    states_in,
    segment_ids,
    positions,
    attention_gain,
    feedforward_gain,
    query_weight,
    keyvalue_weight,
    output_weight,
    route_experts,
    route_weights,
    expert_gateup,
    expert_down,
    cache_slots,
):
    tokens = states_in.shape[0]
    width_share = states_in.shape[1]
    head_rank = lax.axis_index(T)
    group_rank = lax.axis_index(G)
    gain_rows = jnp.zeros((8, width_share), states_in.dtype)
    gain_rows = gain_rows.at[0].set(attention_gain).at[1].set(feedforward_gain)
    packed = jnp.concatenate([states_in, gain_rows], axis=0)
    packed_full = lax.all_gather(packed, T, axis=1, tiled=True)
    states_full = packed_full[:tokens]
    gain_attend = packed_full[tokens]
    gain_forward = packed_full[tokens + 1]
    normed_in = rms_scale(states_full, gain_attend)
    query_cols = query_weight.shape[1]
    keyvalue_heads = keyvalue_weight.shape[1]
    heads_local = query_cols // HD
    piece_rows = query_weight.shape[0]
    weights_packed = jnp.concatenate(
        [query_weight, keyvalue_weight.reshape(piece_rows, -1)], axis=1
    )
    weights_full = gather_rows_over_groups(weights_packed)
    query_full_w = weights_full[:, :query_cols]
    keyvalue_full_w = weights_full[:, query_cols:]
    query_sum = jnp.dot(normed_in, query_full_w, preferred_element_type=jnp.float32)
    keyvalue_sum = jnp.dot(normed_in, keyvalue_full_w, preferred_element_type=jnp.float32)
    queries = rotate(query_sum.reshape(tokens, heads_local, HD), positions).astype(jnp.bfloat16)
    keyvalue_sum = keyvalue_sum.reshape(tokens, keyvalue_heads, 2 * HD)
    key_rows = rotate(keyvalue_sum[..., :HD], positions).astype(jnp.bfloat16)
    value_rows = keyvalue_sum[..., HD:].astype(jnp.bfloat16)
    own_rows = jnp.concatenate([key_rows, value_rows], axis=-1)
    other_rows, other_seg, other_pos = lax.ppermute(
        (own_rows, segment_ids, positions), "c", [(0, 1), (1, 0)]
    )
    all_rows = jnp.concatenate([own_rows, other_rows], axis=0)
    all_seg = jnp.concatenate([segment_ids, other_seg], axis=0)
    all_pos = jnp.concatenate([positions, other_pos], axis=0)
    group_ratio = heads_local // keyvalue_heads
    query_block = queries.reshape(tokens, keyvalue_heads, group_ratio, HD)
    mixed, log_part = attend_block(query_block, segment_ids, positions, all_rows, all_seg, all_pos)
    attended = mixed.reshape(tokens, heads_local * HD)
    log_sums = log_part.reshape(heads_local, tokens)
    partial_value = jnp.dot(attended, output_weight, preferred_element_type=jnp.float32)
    summed = lax.psum(partial_value, T)
    residual = (states_full.astype(jnp.float32) + summed).astype(jnp.bfloat16)
    normed = rms_scale(residual, gain_forward)
    residual_share = lax.dynamic_slice_in_dim(residual, head_rank * width_share, width_share, 1)
    slot_first = head_rank // 2 * expert_gateup.shape[0]
    terms = expert_terms(
        normed, route_experts, route_weights, expert_gateup, expert_down, slot_first
    )
    expert_share = lax.psum_scatter(
        terms.astype(jnp.bfloat16), T, scatter_dimension=1, tiled=True
    ).astype(jnp.float32)
    layer_output = (residual_share.astype(jnp.float32) + expert_share).astype(jnp.bfloat16)
    group_count = lax.axis_size(G)
    per_owner = tokens // group_count
    owners = cache_slots // tokens
    sequence = jnp.arange(tokens, dtype=jnp.int32)
    ordering = jnp.argsort(owners * tokens + sequence)
    send_rows = own_rows[ordering].reshape(group_count, per_owner, keyvalue_heads, 2 * HD)
    send_slots = cache_slots[ordering].reshape(group_count, per_owner)
    got_rows, got_slots = (
        lax.all_to_all(send_rows, G, split_axis=0, concat_axis=0, tiled=True),
        lax.all_to_all(send_slots, G, split_axis=0, concat_axis=0, tiled=True),
    )
    targets = got_slots.reshape(tokens) - group_rank * tokens
    paged_rows = (
        jnp.zeros_like(own_rows).at[targets].set(got_rows.reshape(tokens, keyvalue_heads, 2 * HD))
    )
    return (layer_output, paged_rows, log_sums)


def solution(mesh):
    fine = Mesh(mesh.devices.reshape(8, 2, 2, 2, 4), ("z", "yh", "c", "yl", "x"))
    return jax.shard_map(
        shards,
        mesh=fine,
        in_specs=(
            P(G, T),
            P(G),
            P(G),
            P(T),
            P(T),
            P(G, T),
            P(G, T, None),
            P(T, None),
            P(G, None),
            P(G, None),
            P(T, None, None),
            P(T, None, None),
            P(G),
        ),
        out_specs=(P(G, T), P(G, T, None), P(T, G)),
        check_vma=False,
    )
```

profile of v0, /device:TPU:1, one launch (start us, length us, event | category | flops | bytes accessed | tf_op | source)
XLA Modules:
  0.0 252.0 jit_solution(752531297667724004)
XLA Ops:
  8.1 2.5 collective-permute-start
  10.6 3.0 %collective-permute-start.1 = (bf16[48,320]{1,0:T(8,128)(2,1)S(1)}, bf16[48,320]{1,0:T(8,128)(2,1)S(1)}, u32[]{:S(2)}, u32[]{:S(2)}) collective-permute-start(bf16[48,320]{1,0:T(8,128)(2,1)S(1)} %pad_maximum_fusion.3), channel_id=1, source_target_pairs={{0,64},{32,96},{64,128},{96,160},{128,192},{160,224},{192,0},{224,... | collective-permute-start | bytes 92168 | tf_op jit(solution)/shard_map/ppermute | solution.py:76
  13.6 3.8 %collective-permute-start.2 = (bf16[48,320]{1,0:T(8,128)(2,1)S(1)}, bf16[48,320]{1,0:T(8,128)(2,1)S(1)}, u32[]{:S(2)}, u32[]{:S(2)}) collective-permute-start(bf16[48,320]{1,0:T(8,128)(2,1)S(1)} %pad_maximum_fusion.3), channel_id=1, source_target_pairs={{0,96},{32,128},{64,160},{96,192},{128,224},{160,0},{192,32},{224,... | collective-permute-start | bytes 92168 | tf_op jit(solution)/shard_map/ppermute | solution.py:76
  19.3 1.7 pad_maximum_fusion.1
  21.1 1.7 collective-permute-start.10
  24.7 4.7 %collective-permute-start.4 = (bf16[48,320]{1,0:T(8,128)(2,1)S(1)}, bf16[48,320]{1,0:T(8,128)(2,1)S(1)}, u32[]{:S(2)}, u32[]{:S(2)}) collective-permute-start(bf16[48,320]{1,0:T(8,128)(2,1)S(1)} %pad_maximum_fusion.3), channel_id=1, source_target_pairs={{0,160},{32,192},{64,224},{96,0},{128,32},{160,64},{192,96},{224,1... | collective-permute-start | bytes 92168 | tf_op jit(solution)/shard_map/ppermute | solution.py:76
  30.1 2.5 collective-permute-start.5
  36.2 3.0 %collective-permute-start.7 = (bf16[8,48,320]{2,1,0:T(8,128)(2,1)S(1)}, bf16[8,48,320]{2,1,0:T(8,128)(2,1)S(1)}, u32[]{:S(2)}, u32[]{:S(2)}) collective-permute-start(bf16[8,48,320]{2,1,0:T(8,128)(2,1)S(1)} %broadcast_select_fusion), channel_id=1, source_target_pairs={{0,16},{16,0},{1,17},{17,1},{2,18},{18,2},{3,19},{19,3},{4,20},{20... | collective-permute-start | bytes 737288 | tf_op jit(solution)/shard_map/ppermute | solution.py:80
  40.0 23.9 %collective-permute-done.7 = bf16[8,48,320]{2,1,0:T(8,128)(2,1)S(1)} collective-permute-done((bf16[8,48,320]{2,1,0:T(8,128)(2,1)S(1)}, bf16[8,48,320]{2,1,0:T(8,128)(2,1)S(1)}, u32[]{:S(2)}, u32[]{:S(2)}) %collective-permute-start.7) | collective-permute-done | bytes 245792 | tf_op jit(solution)/shard_map/ppermute | solution.py:80
  66.8 1.1 copy.50
  68.0 2.6 %slice.95 = bf16[512,1536]{0,1:T(8,128)(2,1)} slice(bf16[520,1536]{0,1:T(8,128)(2,1)} %all-gather.2.cloned.1.call-done), slice={[0:512], [0:1536]} | slice | bytes 3145728 | tf_op jit(solution)/shard_map/slice | solution.py:111
  70.6 1.7 copy.59
  72.7 1.5 convert_reduce_fusion
  74.3 2.0 convolution_bitcast_fusion.1
  78.9 1.3 fusion.1
  80.2 1.4 fusion
  81.6 2.0 fusion.19
  83.7 2.3 fusion.54
  86.5 91.7 %all-reduce.3.cloned.1.call-done = f32[512,1536]{1,0:T(8,128)} async-done(((f32[512,1536]{1,0:T(8,128)}), f32[512,1536]{1,0:T(8,128)}) %all-reduce.3.cloned.1.call-update) | async-done | bytes 3145744 | tf_op jit(solution)/shard_map/psum | solution.py:144
  178.2 2.4 fusion.2
  180.6 7.5 %convolution_bitcast_fusion = f32[5,512,512]{2,1,0:T(8,128)S(1)} fusion(bf16[5,1536,512]{2,1,0:T(8,128)(2,1)} %param.27, bf16[512,1536]{1,0:T(8,128)(2,1)S(1)} %get-tuple-element.47, f32[1536]{0:T(1024)S(1)} %get-tuple-element.44, f32[512]{0:T(512)S(1)} %add_rsqrt_fusion), kind=kOutput, calls=%fused_computation.26 | convolution fusion | flops 4029677568 | bytes 14688256 | tf_op jit(solution)/shard_map/td,edf->etf/dot_general | solution.py:62
  188.2 3.5 %multiply_reduce_fusion = bf16[512,1536]{1,0:T(8,128)(2,1)S(1)} fusion(bf16[5,256,1536]{2,1,0:T(8,128)(2,1)S(1)} %copy-done.8, f32[5,512]{1,0:T(8,128)S(1)} %bitcast.103, f32[5,512,512]{2,1,0:T(8,128)S(1)} %convolution_bitcast_fusion), kind=kOutput, calls=%fused_computation.4 | convolution fusion | flops 2024275968 | bytes 10758144 | tf_op jit(solution)/shard_map/etf,efd->etd/dot_general | solution.py:66
  191.7 1.6 copy.57
  193.3 3.8 %sort.17 = (s32[512]{0:T(512)}, s32[512]{0:T(512)S(1)}) sort(s32[512]{0:T(512)S(1)} %fusion.43, s32[512]{0:T(512)S(1)} %iota.31), dimensions={0}, to_apply=%region_8.9 | sort | flops 4608 | bytes 8192 | tf_op jit(solution)/shard_map/jit(argsort)/sort | solution.py:160
  197.1 3.5 %gather_fusion.1 = s32[512]{0:T(512)S(1)} fusion(s32[512]{0:T(512)S(1)} %copy-done.1, s32[1024]{0:T(1024)S(1)} %pad_clamp_fusion), kind=kCustom, calls=%fused_computation.1 | custom fusion | bytes 6144 | tf_op jit(solution)/shard_map/gather | solution.py:162
  201.3 12.2 %all-to-all-start = ((s32[32,1,16]{2,1,0:T(1,128)}), s32[32,1,16]{2,1,0:T(1,128)S(1)}, u32[]{:S(2)}, u32[]{:S(2)}) async-start(s32[32,1,16]{2,1,0:T(1,128)} %bitcast.32), calls=%async_computation | async-start | bytes 32768 | tf_op jit(solution)/shard_map/all_to_all | solution.py:165
  213.5 9.3 %all-to-all-done = s32[32,1,16]{2,1,0:T(1,128)S(1)} async-done(((s32[32,1,16]{2,1,0:T(1,128)}), s32[32,1,16]{2,1,0:T(1,128)S(1)}, u32[]{:S(2)}, u32[]{:S(2)}) %all-to-all-start) | async-done | bytes 2080 | tf_op jit(solution)/shard_map/all_to_all | solution.py:165
  223.1 1.9 gather_fusion.2
  225.0 4.1 %all-to-all-start.1 = ((bf16[32,16,1,128]{3,1,2,0:T(8,128)(2,1)}), bf16[32,16,1,128]{3,1,2,0:T(8,128)(2,1)S(1)}, u32[]{:S(2)}, u32[]{:S(2)}) async-start(bf16[32,16,1,128]{3,1,2,0:T(8,128)(2,1)} %bitcast.36), calls=%async_computation.1 | async-start | bytes 262144 | tf_op jit(solution)/shard_map/all_to_all | solution.py:164
  229.8 10.3 %all-to-all-done.1 = bf16[32,16,1,128]{3,1,2,0:T(8,128)(2,1)S(1)} async-done(((bf16[32,16,1,128]{3,1,2,0:T(8,128)(2,1)}), bf16[32,16,1,128]{3,1,2,0:T(8,128)(2,1)S(1)}, u32[]{:S(2)}, u32[]{:S(2)}) %all-to-all-start.1) | async-done | bytes 131104 | tf_op jit(solution)/shard_map/all_to_all | solution.py:164
  240.1 2.4 scatter_custom_fusion
  243.5 1.2 add_convert_fusion
  (95 shorter events, 19.7 us)
Async XLA Ops:
  7.2 76.5 %copy-start = (bf16[192,1536]{1,0:T(8,128)(2,1)S(1)}, bf16[192,1536]{1,0:T(8,128)(2,1)}, u32[]{:S(2)}) copy-start(bf16[192,1536]{1,0:T(8,128)(2,1)} %param.24) | copy-start | bytes 1769476
  7.2 57.7 %copy-start.7 = (s32[512]{0:T(512)S(1)}, s32[512]{0:T(512)}, u32[]{:S(2)}) copy-start(s32[512]{0:T(512)} %param.18) | copy-start | bytes 6148
  7.2 57.7 %copy-start.4 = (s32[512]{0:T(512)S(1)}, s32[512]{0:T(512)}, u32[]{:S(2)}) copy-start(s32[512]{0:T(512)} %param.19) | copy-start | bytes 6148
  7.2 60.8 %all-gather.2.cloned.1.call-start = ((), (), s32[]{:S(2)}) async-start(), calls=%async_computation.3 | async-start | bytes 2211840 | tf_op jit(solution)/shard_map/all_gather | solution.py:110
  8.1 22.0 %collective-permute-start = (bf16[48,320]{1,0:T(8,128)(2,1)S(1)}, bf16[48,320]{1,0:T(8,128)(2,1)S(1)}, u32[]{:S(2)}, u32[]{:S(2)}) collective-permute-start(bf16[48,320]{1,0:T(8,128)(2,1)S(1)} %pad_maximum_fusion.3), channel_id=1, source_target_pairs={{0,32},{32,64},{64,96},{96,128},{128,160},{160,192},{192,224},{224... | collective-permute-start | bytes 92168 | tf_op jit(solution)/shard_map/ppermute | solution.py:76
  10.6 21.9 %collective-permute-start.1 = (bf16[48,320]{1,0:T(8,128)(2,1)S(1)}, bf16[48,320]{1,0:T(8,128)(2,1)S(1)}, u32[]{:S(2)}, u32[]{:S(2)}) collective-permute-start(bf16[48,320]{1,0:T(8,128)(2,1)S(1)} %pad_maximum_fusion.3), channel_id=1, source_target_pairs={{0,64},{32,96},{64,128},{96,160},{128,192},{160,224},{192,0},{224,... | collective-permute-start | bytes 92168 | tf_op jit(solution)/shard_map/ppermute | solution.py:76
  13.6 19.8 %collective-permute-start.2 = (bf16[48,320]{1,0:T(8,128)(2,1)S(1)}, bf16[48,320]{1,0:T(8,128)(2,1)S(1)}, u32[]{:S(2)}, u32[]{:S(2)}) collective-permute-start(bf16[48,320]{1,0:T(8,128)(2,1)S(1)} %pad_maximum_fusion.3), channel_id=1, source_target_pairs={{0,96},{32,128},{64,160},{96,192},{128,224},{160,0},{192,32},{224,... | collective-permute-start | bytes 92168 | tf_op jit(solution)/shard_map/ppermute | solution.py:76
  17.4 17.0 %collective-permute-start.3 = (bf16[48,320]{1,0:T(8,128)(2,1)S(1)}, bf16[48,320]{1,0:T(8,128)(2,1)S(1)}, u32[]{:S(2)}, u32[]{:S(2)}) collective-permute-start(bf16[48,320]{1,0:T(8,128)(2,1)S(1)} %pad_maximum_fusion.3), channel_id=1, source_target_pairs={{0,128},{32,160},{64,192},{96,224},{128,0},{160,32},{192,64},{224,... | collective-permute-start | bytes 92168 | tf_op jit(solution)/shard_map/ppermute | solution.py:76
  21.0 157.2 %all-reduce.3.cloned.1.call-start = ((), (), s32[]{:S(2)}) async-start(), calls=%async_computation.4 | async-start | bytes 6291456 | tf_op jit(solution)/shard_map/psum | solution.py:144
  21.1 3.6 %collective-permute-start.10 = (s32[512]{0:T(512)}, s32[512]{0:T(512)S(1)}, u32[]{:S(2)}, u32[]{:S(2)}) collective-permute-start(s32[512]{0:T(512)} %param.18), channel_id=1, source_target_pairs={{0,8},{8,0},{1,9},{9,1},{2,10},{10,2},{3,11},{11,3},{4,12},{12,4},... | collective-permute-start | bytes 6152 | tf_op jit(solution)/shard_map/ppermute | solution.py:132
  24.7 9.7 %collective-permute-start.4 = (bf16[48,320]{1,0:T(8,128)(2,1)S(1)}, bf16[48,320]{1,0:T(8,128)(2,1)S(1)}, u32[]{:S(2)}, u32[]{:S(2)}) collective-permute-start(bf16[48,320]{1,0:T(8,128)(2,1)S(1)} %pad_maximum_fusion.3), channel_id=1, source_target_pairs={{0,160},{32,192},{64,224},{96,0},{128,32},{160,64},{192,96},{224,1... | collective-permute-start | bytes 92168 | tf_op jit(solution)/shard_map/ppermute | solution.py:76
  30.1 4.5 %collective-permute-start.5 = (bf16[48,320]{1,0:T(8,128)(2,1)S(1)}, bf16[48,320]{1,0:T(8,128)(2,1)S(1)}, u32[]{:S(2)}, u32[]{:S(2)}) collective-permute-start(bf16[48,320]{1,0:T(8,128)(2,1)S(1)} %pad_maximum_fusion.3), channel_id=1, source_target_pairs={{0,192},{32,224},{64,0},{96,32},{128,64},{160,96},{192,128},{224,1... | collective-permute-start | bytes 92168 | tf_op jit(solution)/shard_map/ppermute | solution.py:76
  32.6 2.9 %collective-permute-start.6 = (bf16[48,320]{1,0:T(8,128)(2,1)S(1)}, bf16[48,320]{1,0:T(8,128)(2,1)S(1)}, u32[]{:S(2)}, u32[]{:S(2)}) collective-permute-start(bf16[48,320]{1,0:T(8,128)(2,1)S(1)} %pad_maximum_fusion.3), channel_id=1, source_target_pairs={{0,224},{32,0},{64,32},{96,64},{128,96},{160,128},{192,160},{224,1... | collective-permute-start | bytes 92168 | tf_op jit(solution)/shard_map/ppermute | solution.py:76
  33.4 5.8 %collective-permute-start.11 = (s32[512]{0:T(512)}, s32[512]{0:T(512)S(1)}, u32[]{:S(2)}, u32[]{:S(2)}) collective-permute-start(s32[512]{0:T(512)} %param.19), channel_id=1, source_target_pairs={{0,8},{8,0},{1,9},{9,1},{2,10},{10,2},{3,11},{11,3},{4,12},{12,4},... | collective-permute-start | bytes 6152 | tf_op jit(solution)/shard_map/ppermute | solution.py:132
  36.2 27.7 %collective-permute-start.7 = (bf16[8,48,320]{2,1,0:T(8,128)(2,1)S(1)}, bf16[8,48,320]{2,1,0:T(8,128)(2,1)S(1)}, u32[]{:S(2)}, u32[]{:S(2)}) collective-permute-start(bf16[8,48,320]{2,1,0:T(8,128)(2,1)S(1)} %broadcast_select_fusion), channel_id=1, source_target_pairs={{0,16},{16,0},{1,17},{17,1},{2,18},{18,2},{3,19},{19,3},{4,20},{20... | collective-permute-start | bytes 737288 | tf_op jit(solution)/shard_map/ppermute | solution.py:80
  64.1 2.4 collective-permute-start.8
  72.3 4.3 %copy-start.3 = (bf16[8,2,2,48,320]{4,3,2,1,0:T(8,128)(2,1)S(1)}, bf16[8,2,2,48,320]{4,3,2,1,0:T(8,128)(2,1)}, u32[]{:S(2)}) copy-start(bf16[8,2,2,48,320]{4,3,2,1,0:T(8,128)(2,1)} %copy.50) | copy-start | bytes 2949124
  77.5 1.4 collective-permute-start.9
  83.7 2.7 %copy-start.5 = (f32[512,8]{0,1:T(8,128)S(1)}, f32[512,8]{0,1:T(8,128)}, u32[]{:S(2)}) copy-start(f32[512,8]{0,1:T(8,128)} %param.26) | copy-start | bytes 49156
  83.7 2.7 %copy-start.6 = (s32[512,8]{0,1:T(8,128)S(1)}, s32[512,8]{0,1:T(8,128)}, u32[]{:S(2)}) copy-start(s32[512,8]{0,1:T(8,128)} %param.25) | copy-start | bytes 49156
  86.0 156.4 %reduce-scatter.4.cloned.1.call-start = ((), (), s32[]{:S(2)}) async-start(), calls=%async_computation.5 | async-start | bytes 1769472
  180.6 7.6 %copy-start.2 = (bf16[512,1536]{1,0:T(8,128)(2,1)}, bf16[512,1536]{1,0:T(8,128)(2,1)S(1)}, u32[]{:S(2)}) copy-start(bf16[512,1536]{1,0:T(8,128)(2,1)S(1)} %get-tuple-element.47) | copy-start | bytes 4718596
  180.6 7.6 %copy-start.8 = (bf16[5,256,1536]{2,1,0:T(8,128)(2,1)S(1)}, bf16[5,256,1536]{2,1,0:T(8,128)(2,1)}, u32[]{:S(2)}) copy-start(bf16[5,256,1536]{2,1,0:T(8,128)(2,1)} %param.28) | copy-start | bytes 11796484
  191.7 1.6 copy-start.1
  201.3 21.6 %all-to-all-start = ((s32[32,1,16]{2,1,0:T(1,128)}), s32[32,1,16]{2,1,0:T(1,128)S(1)}, u32[]{:S(2)}, u32[]{:S(2)}) async-start(s32[32,1,16]{2,1,0:T(1,128)} %bitcast.32), calls=%async_computation | async-start | bytes 32768 | tf_op jit(solution)/shard_map/all_to_all | solution.py:165
  225.0 15.1 %all-to-all-start.1 = ((bf16[32,16,1,128]{3,1,2,0:T(8,128)(2,1)}), bf16[32,16,1,128]{3,1,2,0:T(8,128)(2,1)S(1)}, u32[]{:S(2)}, u32[]{:S(2)}) async-start(bf16[32,16,1,128]{3,1,2,0:T(8,128)(2,1)} %bitcast.36), calls=%async_computation.1 | async-start | bytes 262144 | tf_op jit(solution)/shard_map/all_to_all | solution.py:164
Sparse Core Ops, SparseCore 0:
  21.1 40.3 all-gather.1
  86.2 91.9 all-reduce.2
  193.4 40.6 reduce-scatter.3
where the time goes:
time: 253 us; the launch traced here: 252 us
  waiting for transfers between devices  138 us (55%)
  starting transfers between devices  41.3 us (16%)
  local copies, waits for them, and re-layouts  19.8 us (8%)
  other arithmetic  19.5 us (8%)
  matrix products  19.4 us (8%)
  between operations  14.2 us (6%)
    psum x1, waiting for transfers between devices, shards(): summed = lax.psum(partial_value, T)  91.7 us
    ppermute x1, waiting for transfers between devices, gather_rows_over_groups(): other_y = lax.ppermute(zfull, 'yh', [(0, 1), (1, 0)])  23.9 us
    ppermute x7, starting transfers between devices, gather_rows_over_groups(): got.append(lax.ppermute(block, 'z', [(i, (i + k) % nz) for i in range(nz)]))  17.7 us
    all_to_all x1, starting transfers between devices, shards(): lax.all_to_all(send_slots, G, split_axis=0, concat_axis=0, tiled=True)  12.2 us
    all_to_all x1, waiting for transfers between devices, shards(): lax.all_to_all(send_rows, G, split_axis=0, concat_axis=0, tiled=True)  10.3 us
    all_to_all x1, waiting for transfers between devices, shards(): lax.all_to_all(send_slots, G, split_axis=0, concat_axis=0, tiled=True)  9.3 us
    dot_general x1, matrix products, expert_terms(): jnp.einsum('td,edf->etf', normed, gateup, preferred_element_type=jnp.floa...  7.52 us
    unnamed x28, local copies, waits for them, and re-layouts  5.28 us
  transfers between devices with their start and end apart: 17, of which 8 were waited for; matrix products, arithmetic and copies ran while one was open for 9% of the time, Pallas kernels for 0%

commit v1 on v0

--- a/solution.py
+++ b/solution.py
@@ -141,7 +141,7 @@
     attended = mixed.reshape(tokens, heads_local * HD)
     log_sums = log_part.reshape(heads_local, tokens)
     partial_value = jnp.dot(attended, output_weight, preferred_element_type=jnp.float32)
-    summed = lax.psum(partial_value, T)
+    summed = lax.psum(lax.psum(partial_value, "x"), "yl")
     residual = (states_full.astype(jnp.float32) + summed).astype(jnp.bfloat16)
     normed = rms_scale(residual, gain_forward)
     residual_share = lax.dynamic_slice_in_dim(residual, head_rank * width_share, width_share, 1)

time: 253 us -> 338 us (1.34)
  waiting for transfers between devices: 138 us -> 225 us
    psum x1 -> x2, waiting for transfers between devices: 91.7 us -> 179 us  [shards(): summed = lax.psum(lax.psum(partial_value, 'x'), 'yl')]
  transfers between devices with their start and end apart: 17 -> 18, of which waited for: 8 -> 9; matrix products, arithmetic and copies ran while one was open for 9% -> 7% of each run, Pallas kernels for 0% -> 0%
where the time goes in v1:
time: 338 us; the launch traced here: 337 us
  waiting for transfers between devices  225 us (67%)
  starting transfers between devices  39.1 us (12%)
  local copies, waits for them, and re-layouts  19.8 us (6%)
  other arithmetic  19.5 us (6%)
  matrix products  19.4 us (6%)
  between operations  14.2 us (4%)
    psum x2, waiting for transfers between devices, shards(): summed = lax.psum(lax.psum(partial_value, 'x'), 'yl')  179 us
    ppermute x1, waiting for transfers between devices, gather_rows_over_groups(): other_y = lax.ppermute(zfull, 'yh', [(0, 1), (1, 0)])  23.9 us
    ppermute x7, starting transfers between devices, gather_rows_over_groups(): got.append(lax.ppermute(block, 'z', [(i, (i + k) % nz) for i in range(nz)]))  17.7 us
    all_to_all x1, waiting for transfers between devices, shards(): lax.all_to_all(send_rows, G, split_axis=0, concat_axis=0, tiled=True)  10.4 us
    all_to_all x1, starting transfers between devices, shards(): lax.all_to_all(send_slots, G, split_axis=0, concat_axis=0, tiled=True)  9.99 us
    all_to_all x1, waiting for transfers between devices, shards(): lax.all_to_all(send_slots, G, split_axis=0, concat_axis=0, tiled=True)  9.28 us
    dot_general x1, matrix products, expert_terms(): jnp.einsum('td,edf->etf', normed, gateup, preferred_element_type=jnp.floa...  7.51 us
  transfers between devices with their start and end apart: 18, of which 9 were waited for; matrix products, arithmetic and copies ran while one was open for 7% of the time, Pallas kernels for 0%

profile of v1, /device:TPU:1, one launch (start us, length us, event | category | flops | bytes accessed | tf_op | source)
XLA Modules:
  0.0 337.2 jit_solution(14730869390227129197)
XLA Ops:
  8.1 2.5 collective-permute-start
  10.6 3.0 collective-permute-start.1
  13.6 3.8 %collective-permute-start.2 = (bf16[48,320]{1,0:T(8,128)(2,1)S(1)}, bf16[48,320]{1,0:T(8,128)(2,1)S(1)}, u32[]{:S(2)}, u32[]{:S(2)}) collective-permute-start(bf16[48,320]{1,0:T(8,128)(2,1)S(1)} %pad_maximum_fusion.3), channel_id=1, source_target_pairs={{0,96},{32,128},{64,160},{96,192},{128,224},{160,0},{192,32},{224,... | collective-permute-start | bytes 92168 | tf_op jit(solution)/shard_map/ppermute | solution.py:76
  19.3 1.7 pad_maximum_fusion.1
  21.1 1.7 collective-permute-start.10
  24.7 4.7 %collective-permute-start.4 = (bf16[48,320]{1,0:T(8,128)(2,1)S(1)}, bf16[48,320]{1,0:T(8,128)(2,1)S(1)}, u32[]{:S(2)}, u32[]{:S(2)}) collective-permute-start(bf16[48,320]{1,0:T(8,128)(2,1)S(1)} %pad_maximum_fusion.3), channel_id=1, source_target_pairs={{0,160},{32,192},{64,224},{96,0},{128,32},{160,64},{192,96},{224,1... | collective-permute-start | bytes 92168 | tf_op jit(solution)/shard_map/ppermute | solution.py:76
  30.1 2.5 collective-permute-start.5
  36.2 3.0 collective-permute-start.7
  40.0 23.9 %collective-permute-done.7 = bf16[8,48,320]{2,1,0:T(8,128)(2,1)S(1)} collective-permute-done((bf16[8,48,320]{2,1,0:T(8,128)(2,1)S(1)}, bf16[8,48,320]{2,1,0:T(8,128)(2,1)S(1)}, u32[]{:S(2)}, u32[]{:S(2)}) %collective-permute-start.7) | collective-permute-done | bytes 245792 | tf_op jit(solution)/shard_map/ppermute | solution.py:80
  68.0 2.6 slice.95
  70.6 1.7 copy.59
  72.7 1.5 convert_reduce_fusion
  74.3 2.0 convolution_bitcast_fusion.1
  78.9 1.3 fusion.1
  80.2 1.4 fusion
  81.6 2.0 fusion.19
  83.7 2.3 fusion.54
  86.1 79.6 %all-reduce.4.cloned.1.call-done = f32[512,1536]{1,0:T(8,128)} async-done(((f32[512,1536]{1,0:T(8,128)}), f32[512,1536]{1,0:T(8,128)}) %all-reduce.4.cloned.1.call-update) | async-done | bytes 3145744 | tf_op jit(solution)/shard_map/psum | solution.py:144
  166.1 99.6 %all-reduce.6.cloned.1.call-done = f32[512,1536]{1,0:T(8,128)} async-done(((f32[512,1536]{1,0:T(8,128)}), f32[512,1536]{1,0:T(8,128)}) %all-reduce.6.cloned.1.call-update) | async-done | bytes 3145744 | tf_op jit(solution)/shard_map/psum | solution.py:144
  265.7 2.4 fusion.2
  268.1 7.5 %convolution_bitcast_fusion = f32[5,512,512]{2,1,0:T(8,128)S(1)} fusion(bf16[5,1536,512]{2,1,0:T(8,128)(2,1)} %param.27, bf16[512,1536]{1,0:T(8,128)(2,1)S(1)} %get-tuple-element.47, f32[1536]{0:T(1024)S(1)} %get-tuple-element.44, f32[512]{0:T(512)S(1)} %add_rsqrt_fusion), kind=kOutput, calls=%fused_computation.26 | convolution fusion | flops 4029677568 | bytes 14688256 | tf_op jit(solution)/shard_map/td,edf->etf/dot_general | solution.py:62
  275.6 3.5 %multiply_reduce_fusion = bf16[512,1536]{1,0:T(8,128)(2,1)S(1)} fusion(bf16[5,256,1536]{2,1,0:T(8,128)(2,1)S(1)} %copy-done.8, f32[5,512]{1,0:T(8,128)S(1)} %bitcast.103, f32[5,512,512]{2,1,0:T(8,128)S(1)} %convolution_bitcast_fusion), kind=kOutput, calls=%fused_computation.4 | convolution fusion | flops 2024275968 | bytes 10758144 | tf_op jit(solution)/shard_map/etf,efd->etd/dot_general | solution.py:66
  279.1 1.6 copy.57
  280.8 3.8 %sort.17 = (s32[512]{0:T(512)}, s32[512]{0:T(512)S(1)}) sort(s32[512]{0:T(512)S(1)} %fusion.43, s32[512]{0:T(512)S(1)} %iota.31), dimensions={0}, to_apply=%region_9.10 | sort | flops 4608 | bytes 8192 | tf_op jit(solution)/shard_map/jit(argsort)/sort | solution.py:160
  284.6 3.5 %gather_fusion.1 = s32[512]{0:T(512)S(1)} fusion(s32[512]{0:T(512)S(1)} %copy-done.1, s32[1024]{0:T(1024)S(1)} %pad_clamp_fusion), kind=kCustom, calls=%fused_computation.1 | custom fusion | bytes 6144 | tf_op jit(solution)/shard_map/gather | solution.py:162
  288.8 10.0 %all-to-all-start = ((s32[32,1,16]{2,1,0:T(1,128)}), s32[32,1,16]{2,1,0:T(1,128)S(1)}, u32[]{:S(2)}, u32[]{:S(2)}) async-start(s32[32,1,16]{2,1,0:T(1,128)} %bitcast.32), calls=%async_computation | async-start | bytes 32768 | tf_op jit(solution)/shard_map/all_to_all | solution.py:165
  298.8 9.3 %all-to-all-done = s32[32,1,16]{2,1,0:T(1,128)S(1)} async-done(((s32[32,1,16]{2,1,0:T(1,128)}), s32[32,1,16]{2,1,0:T(1,128)S(1)}, u32[]{:S(2)}, u32[]{:S(2)}) %all-to-all-start) | async-done | bytes 2080 | tf_op jit(solution)/shard_map/all_to_all | solution.py:165
  308.3 1.9 gather_fusion.2
  310.2 4.1 %all-to-all-start.1 = ((bf16[32,16,1,128]{3,1,2,0:T(8,128)(2,1)}), bf16[32,16,1,128]{3,1,2,0:T(8,128)(2,1)S(1)}, u32[]{:S(2)}, u32[]{:S(2)}) async-start(bf16[32,16,1,128]{3,1,2,0:T(8,128)(2,1)} %bitcast.36), calls=%async_computation.1 | async-start | bytes 262144 | tf_op jit(solution)/shard_map/all_to_all | solution.py:164
  315.0 10.4 %all-to-all-done.1 = bf16[32,16,1,128]{3,1,2,0:T(8,128)(2,1)S(1)} async-done(((bf16[32,16,1,128]{3,1,2,0:T(8,128)(2,1)}), bf16[32,16,1,128]{3,1,2,0:T(8,128)(2,1)S(1)}, u32[]{:S(2)}, u32[]{:S(2)}) %all-to-all-start.1) | async-done | bytes 131104 | tf_op jit(solution)/shard_map/all_to_all | solution.py:164
  325.3 2.4 scatter_custom_fusion
  328.7 1.2 add_convert_fusion
  (98 shorter events, 20.9 us)
Async XLA Ops:
  7.2 76.5 %copy-start = (bf16[192,1536]{1,0:T(8,128)(2,1)S(1)}, bf16[192,1536]{1,0:T(8,128)(2,1)}, u32[]{:S(2)}) copy-start(bf16[192,1536]{1,0:T(8,128)(2,1)} %param.24) | copy-start | bytes 1769476
  7.2 57.7 %copy-start.7 = (s32[512]{0:T(512)S(1)}, s32[512]{0:T(512)}, u32[]{:S(2)}) copy-start(s32[512]{0:T(512)} %param.18) | copy-start | bytes 6148
  7.2 57.7 %copy-start.4 = (s32[512]{0:T(512)S(1)}, s32[512]{0:T(512)}, u32[]{:S(2)}) copy-start(s32[512]{0:T(512)} %param.19) | copy-start | bytes 6148
  7.2 60.8 %all-gather.2.cloned.1.call-start = ((), (), s32[]{:S(2)}) async-start(), calls=%async_computation.3 | async-start | bytes 2211840 | tf_op jit(solution)/shard_map/all_gather | solution.py:110
  8.1 22.0 %collective-permute-start = (bf16[48,320]{1,0:T(8,128)(2,1)S(1)}, bf16[48,320]{1,0:T(8,128)(2,1)S(1)}, u32[]{:S(2)}, u32[]{:S(2)}) collective-permute-start(bf16[48,320]{1,0:T(8,128)(2,1)S(1)} %pad_maximum_fusion.3), channel_id=1, source_target_pairs={{0,32},{32,64},{64,96},{96,128},{128,160},{160,192},{192,224},{224... | collective-permute-start | bytes 92168 | tf_op jit(solution)/shard_map/ppermute | solution.py:76
  10.6 21.9 %collective-permute-start.1 = (bf16[48,320]{1,0:T(8,128)(2,1)S(1)}, bf16[48,320]{1,0:T(8,128)(2,1)S(1)}, u32[]{:S(2)}, u32[]{:S(2)}) collective-permute-start(bf16[48,320]{1,0:T(8,128)(2,1)S(1)} %pad_maximum_fusion.3), channel_id=1, source_target_pairs={{0,64},{32,96},{64,128},{96,160},{128,192},{160,224},{192,0},{224,... | collective-permute-start | bytes 92168 | tf_op jit(solution)/shard_map/ppermute | solution.py:76
  13.6 19.8 %collective-permute-start.2 = (bf16[48,320]{1,0:T(8,128)(2,1)S(1)}, bf16[48,320]{1,0:T(8,128)(2,1)S(1)}, u32[]{:S(2)}, u32[]{:S(2)}) collective-permute-start(bf16[48,320]{1,0:T(8,128)(2,1)S(1)} %pad_maximum_fusion.3), channel_id=1, source_target_pairs={{0,96},{32,128},{64,160},{96,192},{128,224},{160,0},{192,32},{224,... | collective-permute-start | bytes 92168 | tf_op jit(solution)/shard_map/ppermute | solution.py:76
  17.4 17.0 %collective-permute-start.3 = (bf16[48,320]{1,0:T(8,128)(2,1)S(1)}, bf16[48,320]{1,0:T(8,128)(2,1)S(1)}, u32[]{:S(2)}, u32[]{:S(2)}) collective-permute-start(bf16[48,320]{1,0:T(8,128)(2,1)S(1)} %pad_maximum_fusion.3), channel_id=1, source_target_pairs={{0,128},{32,160},{64,192},{96,224},{128,0},{160,32},{192,64},{224,... | collective-permute-start | bytes 92168 | tf_op jit(solution)/shard_map/ppermute | solution.py:76
  21.0 144.6 %all-reduce.4.cloned.1.call-start = ((), (), s32[]{:S(2)}) async-start(), calls=%async_computation.4 | async-start | bytes 6291456 | tf_op jit(solution)/shard_map/psum | solution.py:144
  21.1 3.6 %collective-permute-start.10 = (s32[512]{0:T(512)}, s32[512]{0:T(512)S(1)}, u32[]{:S(2)}, u32[]{:S(2)}) collective-permute-start(s32[512]{0:T(512)} %param.18), channel_id=1, source_target_pairs={{0,8},{8,0},{1,9},{9,1},{2,10},{10,2},{3,11},{11,3},{4,12},{12,4},... | collective-permute-start | bytes 6152 | tf_op jit(solution)/shard_map/ppermute | solution.py:132
  24.7 9.7 %collective-permute-start.4 = (bf16[48,320]{1,0:T(8,128)(2,1)S(1)}, bf16[48,320]{1,0:T(8,128)(2,1)S(1)}, u32[]{:S(2)}, u32[]{:S(2)}) collective-permute-start(bf16[48,320]{1,0:T(8,128)(2,1)S(1)} %pad_maximum_fusion.3), channel_id=1, source_target_pairs={{0,160},{32,192},{64,224},{96,0},{128,32},{160,64},{192,96},{224,1... | collective-permute-start | bytes 92168 | tf_op jit(solution)/shard_map/ppermute | solution.py:76
  30.1 4.5 %collective-permute-start.5 = (bf16[48,320]{1,0:T(8,128)(2,1)S(1)}, bf16[48,320]{1,0:T(8,128)(2,1)S(1)}, u32[]{:S(2)}, u32[]{:S(2)}) collective-permute-start(bf16[48,320]{1,0:T(8,128)(2,1)S(1)} %pad_maximum_fusion.3), channel_id=1, source_target_pairs={{0,192},{32,224},{64,0},{96,32},{128,64},{160,96},{192,128},{224,1... | collective-permute-start | bytes 92168 | tf_op jit(solution)/shard_map/ppermute | solution.py:76
  32.6 2.9 collective-permute-start.6
  33.4 5.8 %collective-permute-start.11 = (s32[512]{0:T(512)}, s32[512]{0:T(512)S(1)}, u32[]{:S(2)}, u32[]{:S(2)}) collective-permute-start(s32[512]{0:T(512)} %param.19), channel_id=1, source_target_pairs={{0,8},{8,0},{1,9},{9,1},{2,10},{10,2},{3,11},{11,3},{4,12},{12,4},... | collective-permute-start | bytes 6152 | tf_op jit(solution)/shard_map/ppermute | solution.py:132
  36.2 27.7 %collective-permute-start.7 = (bf16[8,48,320]{2,1,0:T(8,128)(2,1)S(1)}, bf16[8,48,320]{2,1,0:T(8,128)(2,1)S(1)}, u32[]{:S(2)}, u32[]{:S(2)}) collective-permute-start(bf16[8,48,320]{2,1,0:T(8,128)(2,1)S(1)} %broadcast_select_fusion), channel_id=1, source_target_pairs={{0,16},{16,0},{1,17},{17,1},{2,18},{18,2},{3,19},{19,3},{4,20},{20... | collective-permute-start | bytes 737288 | tf_op jit(solution)/shard_map/ppermute | solution.py:80
  64.1 2.4 collective-permute-start.8
  72.3 4.3 %copy-start.3 = (bf16[8,2,2,48,320]{4,3,2,1,0:T(8,128)(2,1)S(1)}, bf16[8,2,2,48,320]{4,3,2,1,0:T(8,128)(2,1)}, u32[]{:S(2)}) copy-start(bf16[8,2,2,48,320]{4,3,2,1,0:T(8,128)(2,1)} %copy.50) | copy-start | bytes 2949124
  77.5 1.4 collective-permute-start.9
  86.0 80.0 %copy-start.5 = (f32[512,8]{0,1:T(8,128)S(1)}, f32[512,8]{0,1:T(8,128)}, u32[]{:S(2)}) copy-start(f32[512,8]{0,1:T(8,128)} %param.26) | copy-start | bytes 49156
  86.0 80.0 %copy-start.6 = (s32[512,8]{0,1:T(8,128)S(1)}, s32[512,8]{0,1:T(8,128)}, u32[]{:S(2)}) copy-start(s32[512,8]{0,1:T(8,128)} %param.25) | copy-start | bytes 49156
  86.0 179.6 %all-reduce.6.cloned.1.call-start = ((), (), s32[]{:S(2)}) async-start(), calls=%async_computation.5 | async-start | bytes 6291456 | tf_op jit(solution)/shard_map/psum | solution.py:144
  165.7 162.0 %reduce-scatter.4.cloned.1.call-start = ((), (), s32[]{:S(2)}) async-start(), calls=%async_computation.6 | async-start | bytes 1769472
  268.1 7.6 %copy-start.2 = (bf16[512,1536]{1,0:T(8,128)(2,1)}, bf16[512,1536]{1,0:T(8,128)(2,1)S(1)}, u32[]{:S(2)}) copy-start(bf16[512,1536]{1,0:T(8,128)(2,1)S(1)} %get-tuple-element.47) | copy-start | bytes 4718596
  268.1 7.5 %copy-start.8 = (bf16[5,256,1536]{2,1,0:T(8,128)(2,1)S(1)}, bf16[5,256,1536]{2,1,0:T(8,128)(2,1)}, u32[]{:S(2)}) copy-start(bf16[5,256,1536]{2,1,0:T(8,128)(2,1)} %param.28) | copy-start | bytes 11796484
  279.1 1.6 copy-start.1
  288.8 19.3 %all-to-all-start = ((s32[32,1,16]{2,1,0:T(1,128)}), s32[32,1,16]{2,1,0:T(1,128)S(1)}, u32[]{:S(2)}, u32[]{:S(2)}) async-start(s32[32,1,16]{2,1,0:T(1,128)} %bitcast.32), calls=%async_computation | async-start | bytes 32768 | tf_op jit(solution)/shard_map/all_to_all | solution.py:165
  310.2 15.1 %all-to-all-start.1 = ((bf16[32,16,1,128]{3,1,2,0:T(8,128)(2,1)}), bf16[32,16,1,128]{3,1,2,0:T(8,128)(2,1)S(1)}, u32[]{:S(2)}, u32[]{:S(2)}) async-start(bf16[32,16,1,128]{3,1,2,0:T(8,128)(2,1)} %bitcast.36), calls=%async_computation.1 | async-start | bytes 262144 | tf_op jit(solution)/shard_map/all_to_all | solution.py:164
Sparse Core Ops, SparseCore 0:
  21.1 40.3 all-gather.1
  86.1 79.4 all-reduce.3
  168.2 97.3 all-reduce.5
  280.9 39.8 reduce-scatter.3
